TPU v7x, 512 devices: a whole 4x8x8 slice. The times are simulated.
512 devices in a mesh: gx: 8 (over y), gy: 64 (over z, x, core).
Axes of the slice: x: 4, y: 8, z: 8, core: 2. Of those that a mesh axis runs over, the one named last changes fastest.
Arguments:
- source: float32 [512, 256, 128], P('gy', 'gx'), may hold values from -0.004 to 0.004
- mask: int32 [512, 256, 128], P('gy', 'gx'), may hold values from 0 to 2, as said below
- cond_x: float32 [512, 256, 128], P('gy', 'gx'), may hold values from 0.0012 to 0.06
- cond_y: float32 [512, 256, 128], P('gy', 'gx'), may hold values from 0.4 to 5
- cond_z: float32 [512, 256, 128], P('gy', 'gx'), may hold values from 0.0004 to 0.01
Outputs:
- solution: float32 [512, 256, 128], P('gy', 'gx')
Inputs may be any that keep to these rules, and one draw needn't show every extreme that they name: `mask`: 0 marks a fluid cell, 1 a cut cell, 2 a solid cell.
All inputs are finite; a program needn't handle non-finite values.
Results may differ from a plain program's by a relative error of at most 0.00095.
Values sent between devices are 32-bit elements; how exact they have to be, the bound alone decides.
No kernel may reach another device: no remote copies, remote signals or barrier semaphores. Data moves between devices by JAX's collectives and lax.ppermute only.
A program may use at most 128 MiB of HBM per device.

v0:
```python
import jax
import jax.numpy as jnp
from jax import lax
from jax.sharding import Mesh
from jax.sharding import PartitionSpec as P

LEVELS = 6
GY = ("gy_0", "gy_1", "gy_2")
base_shift = 0.001
wall_term = 0.02


def in_blocks(x, dim, count):
    before, after = (x.shape[:dim], x.shape[dim + 1 :])
    return jnp.moveaxis(x.reshape(*before, count, -1, *after), dim, 0)


def in_order(parts, dim):
    parts = jnp.moveaxis(parts, 0, dim)
    shape = parts.shape
    return parts.reshape(*shape[:dim], shape[dim] * shape[dim + 1], *shape[dim + 2 :])


def turned_blocks(parts, axes, sequence):
    shape = [lax.axis_size(a) for a in axes]
    parts = parts.reshape(*shape, *parts.shape[1:])
    for k in sequence:
        parts = lax.all_to_all(parts, axes[k], split_axis=k, concat_axis=k, tiled=True)
    return parts.reshape(-1, *parts.shape[len(axes) :])


def exchange_by_chip(x, groups, sequence, split_dim, concat_dim):
    count = lax.axis_size(groups[0]) * lax.axis_size(groups[1])
    parts = in_blocks(x, split_dim, count)
    return in_order(turned_blocks(parts, groups, sequence), concat_dim)


def copy_for_each(x, axis):
    count = lax.axis_size(axis)
    return lax.all_to_all(jnp.broadcast_to(x[None], (count, *x.shape)), axis, 0, 0, tiled=True)


def gather_directly(x, axis, dim):
    parts = copy_for_each(x, axis)
    return in_order(parts, dim)


def padded(cells, sides, width):
    for axis, dim in sides:
        count = lax.axis_size(axis)
        ends = count - 1
        head = lax.slice_in_dim(cells, 0, width, axis=dim)
        tail = lax.slice_in_dim(cells, cells.shape[dim] - width, cells.shape[dim], axis=dim)
        cells = jnp.concatenate(
            [
                lax.ppermute(tail, axis, [(i, (i + 1) % count) for i in range(ends)]),
                cells,
                lax.ppermute(head, axis, [((i + 1) % count, i) for i in range(ends)]),
            ],
            axis=dim,
        )
    return cells


def with_halo(x, sides, width):
    edges = {}
    for axis, dim in sides:
        count, length = (lax.axis_size(axis), x.shape[dim])
        up = [(i, (i + 1) % count) for i in range(count - 1)]
        last = lax.slice_in_dim(x, length - width, length, axis=dim)
        leading = lax.slice_in_dim(x, 0, width, axis=dim)
        edges[dim] = (
            lax.ppermute(last, axis, up),
            lax.ppermute(leading, axis, [(b, a) for a, b in up]),
        )
    done = []
    for _, dim in sides:
        low, high = edges[dim]
        around = [(width, width) if d in done else (0, 0) for d in range(x.ndim)]
        x = jnp.concatenate([jnp.pad(low, around), x, jnp.pad(high, around)], axis=dim)
        done.append(dim)
    return x


def swapped(x, axis, stride):
    return lax.ppermute(x, axis, [(i, i ^ 1 << stride) for i in range(lax.axis_size(axis))])


def ahead(field, axis):
    size = field.shape[axis]
    edge = jnp.zeros_like(lax.slice_in_dim(field, 0, 1, axis=axis))
    return jnp.concatenate([lax.slice_in_dim(field, 1, size, axis=axis), edge], axis=axis)


def behind(field, axis):
    size = field.shape[axis]
    edge = jnp.zeros_like(lax.slice_in_dim(field, 0, 1, axis=axis))
    return jnp.concatenate([edge, lax.slice_in_dim(field, 0, size - 1, axis=axis)], axis=axis)


def coarse_sum(field):
    depth, width, height = field.shape
    return field.reshape(depth // 2, 2, width // 2, 2, height // 2, 2).sum(axis=(1, 3, 5))


def coarse_face(face, axis, parity):
    picked = lax.slice_in_dim(face, parity, face.shape[axis], stride=2, axis=axis)
    return 0.125 * coarse_sum(jnp.repeat(picked, 2, axis=axis))


def prolong(field):
    return jnp.repeat(jnp.repeat(jnp.repeat(field, 2, axis=0), 2, axis=1), 2, axis=2)


def upper_flag(bit):
    return lax.axis_index(GY) // 2**bit % 2


def line_factors(lower, diag, upper):
    denoms = [diag[0]]
    ratios = [upper[0] / diag[0]]
    for place in range(1, diag.shape[0]):
        pivot = diag[place] - lower[place] * ratios[place - 1]
        denoms.append(pivot)
        ratios.append(upper[place] / pivot)
    return (denoms, ratios)


def rows_solve(level, rhs):
    lower = level["lower"]
    denoms = level["denoms"]
    ratios = level["ratios"]
    count = rhs.shape[0]
    values = [rhs[0] / denoms[0]]
    for place in range(1, count):
        values.append((rhs[place] - lower[place] * values[place - 1]) / denoms[place])
    result = [values[count - 1]]
    for place in range(count - 2, -1, -1):
        result.append(values[place] - ratios[place] * result[-1])
    return jnp.stack(result[::-1])


def assemble(faces, group):
    face_x, low_x, face_y, low_y, face_z, shift = faces
    low_z = behind(face_z, 2)
    diag = shift + face_x + low_x + face_y + low_y + face_z + low_z
    level = {
        "face_x": face_x,
        "low_x": low_x,
        "face_y": face_y,
        "low_y": low_y,
        "face_z": face_z,
        "low_z": low_z,
        "diag": diag,
        "group": group,
    }
    level["lower"] = -low_y
    denoms, ratios = line_factors(-low_y, diag, -face_y)
    level["denoms"] = denoms
    level["ratios"] = ratios
    blank = jnp.zeros_like(diag)
    level["first_resp"] = rows_solve(level, blank.at[0].set(1.0))
    level["last_resp"] = rows_solve(level, blank.at[-1].set(1.0))
    level["alpha"] = low_y[0] * level["first_resp"][0]
    level["gamma"] = low_y[0] * level["first_resp"][-1]
    level["beta"] = face_y[-1] * level["last_resp"][0]
    level["delta"] = face_y[-1] * level["last_resp"][-1]
    return level


def forward_terms(alpha, beta, gamma, delta, head, tail):
    zeros = jnp.zeros_like(head)
    ones = jnp.ones_like(head)
    return (
        gamma * beta - alpha * delta,
        zeros,
        delta,
        gamma * head - alpha * tail,
        gamma,
        tail,
        -alpha,
        zeros,
        ones,
    )


def chain_forward(earlier, later):
    product = []
    for left_row in range(3):
        for column in range(3):
            product.append(
                later[3 * left_row] * earlier[column]
                + later[3 * left_row + 1] * earlier[3 + column]
                + later[3 * left_row + 2] * earlier[6 + column]
            )
    scale = product[8]
    return tuple((entry / scale for entry in product))


def chain_backward(earlier, later):
    return (later[0] + later[1] * earlier[0], later[1] * earlier[1])


def settle(alpha, beta, head, state):
    carry_q = state[2] / state[8]
    carry_p = state[5] / state[8]
    pivot = 1.0 - alpha * carry_q
    return ((head + alpha * carry_p) / pivot, beta / pivot, carry_q, carry_p)


def reduced_local(alpha, beta, gamma, delta, head, tail):
    zeros = jnp.zeros_like(head[:1])
    ones = jnp.ones_like(head[:1])
    identity = (ones, zeros, zeros, zeros, ones, zeros, zeros, zeros, ones)
    terms = forward_terms(alpha, beta, gamma, delta, head, tail)
    inclusive = lax.associative_scan(chain_forward, terms, axis=0)
    state = tuple(
        (jnp.concatenate([plain, entry[:-1]], axis=0) for plain, entry in zip(identity, inclusive))
    )
    start, slope, carry_q, carry_p = settle(alpha, beta, head, state)
    later = lax.associative_scan(chain_backward, (start, slope), reverse=True, axis=0)
    next_first = jnp.concatenate([later[0][1:], zeros], axis=0)
    first = start + slope * next_first
    return (carry_p + carry_q * first, next_first)


def pick_block(values, index, shape):
    return lax.dynamic_index_in_dim(values, index, 0, keepdims=False).reshape(shape)


def reduced_moved(level, head, tail):
    group = level["group"]
    shape = head.shape
    packed = jnp.stack(
        [level["alpha"], level["beta"], level["gamma"], level["delta"], head, tail]
    ).reshape(6, 1, -1)
    if group == 1:
        moved = exchange_by_chip(packed, (("gy_0", "gy_1"), "gy_2"), (1, 0), 2, 1)
        prev_last, next_first = reduced_local(
            moved[0], moved[1], moved[2], moved[3], moved[4], moved[5]
        )
        back = lax.all_to_all(
            jnp.stack([prev_last, next_first]), GY, split_axis=1, concat_axis=2, tiled=True
        )
        return (back[0, 0].reshape(shape), back[1, 0].reshape(shape))
    whole = gather_directly(packed, GY, 1)
    whole = whole.reshape(6, whole.shape[1] // group, group, -1)[:, :, 0]
    prev_last, next_first = reduced_local(
        whole[0], whole[1], whole[2], whole[3], whole[4], whole[5]
    )
    index = lax.axis_index(GY) // group
    return (pick_block(prev_last, index, shape), pick_block(next_first, index, shape))


def line_solve(level, rhs):
    local = rows_solve(level, rhs)
    prev_last, next_first = reduced_moved(level, local[0], local[-1])
    return (
        local
        + (level["low_y"][0] * prev_last)[None] * level["first_resp"]
        + (level["face_y"][-1] * next_first)[None] * level["last_resp"]
    )


def neighbour_terms(level, field):
    rim = padded(field, (("gx", 1),), 1)
    return (
        level["face_x"] * rim[:, 2:]
        + level["low_x"] * rim[:, :-2]
        + level["face_z"] * ahead(field, 2)
        + level["low_z"] * behind(field, 2)
    )


def relax(level, field, rhs):
    return line_solve(level, rhs + neighbour_terms(level, field))


WHOLE_FROM = 3


def gather_whole(block, depth):
    if depth == 2:
        axes, count = (("gx",) + GY, lax.axis_size(GY))
    else:
        axes, count = (("gx", "gy_0", "gy_1"), lax.axis_size(GY) // 2)
    parts = lax.all_gather(block, axes, axis=0)
    parts = parts.reshape(lax.axis_size("gx"), count, *block.shape)
    parts = jnp.moveaxis(parts, (0, 1), (3, 1))
    lead, rows, width, height = (block.shape[0], block.shape[1], block.shape[2], block.shape[3])
    return parts.reshape(lead, count * rows, lax.axis_size("gx") * width, height)


def whole_level(face_x, face_y, face_z, shift):
    low_x = behind(face_x, 1)
    low_y = behind(face_y, 0)
    low_z = behind(face_z, 2)
    diag = shift + face_x + low_x + face_y + low_y + face_z + low_z
    level = {
        "face_x": face_x,
        "low_x": low_x,
        "face_y": face_y,
        "low_y": low_y,
        "face_z": face_z,
        "low_z": low_z,
        "diag": diag,
        "lower": -low_y,
    }
    level["denoms"], level["ratios"] = line_factors(-low_y, diag, -face_y)
    return level


def whole_terms(level, field):
    return (
        level["face_x"] * ahead(field, 1)
        + level["low_x"] * behind(field, 1)
        + level["face_z"] * ahead(field, 2)
        + level["low_z"] * behind(field, 2)
    )


def whole_cycle(levels, depth, rhs):
    level = levels[depth]
    field = rows_solve(level, rhs)
    if depth == len(levels) - 1:
        return rows_solve(level, rhs + whole_terms(level, field))
    residual = whole_terms(level, field)
    correction = whole_cycle(levels, depth + 1, 0.25 * coarse_sum(residual))
    field = field + prolong(correction)
    return rows_solve(level, rhs + whole_terms(level, field))


def body(source, mask, cond_x, cond_y, cond_z):
    open_cells = (mask != 2).astype(jnp.float32)
    wall = (mask == 1).astype(jnp.float32)
    rim = with_halo(
        jnp.stack([cond_x * open_cells, cond_y * open_cells, open_cells]), (("gx", 2), (GY, 1)), 1
    )
    faces = (
        cond_x * open_cells * rim[2, 1:-1, 2:],
        rim[0, 1:-1, :-2] * open_cells,
        cond_y * open_cells * rim[2, 2:, 1:-1],
        rim[1, :-2, 1:-1] * open_cells,
        cond_z * open_cells * ahead(open_cells, 2),
        base_shift + wall_term * wall,
    )
    rhs = source * open_cells
    levels = []
    fields = []
    sources = []
    residual = rhs
    for depth in range(WHOLE_FROM):
        group = 1
        if depth > 0:
            face_x, low_x, face_y, low_y, face_z, shift = faces
            faces = (
                coarse_face(face_x, 1, 1),
                coarse_face(low_x, 1, 0),
                coarse_face(face_y, 0, 1),
                coarse_face(low_y, 0, 0),
                coarse_face(face_z, 2, 1),
                0.25 * coarse_sum(shift),
            )
            rhs = 0.25 * coarse_sum(residual)
            if depth >= 2:
                group = 2 ** (depth - 1)
                stacked = jnp.stack((rhs,) + faces)
                partner = swapped(stacked, GY, depth - 2)
                upper = upper_flag(depth - 2) == 1
                folded = jnp.concatenate(
                    [jnp.where(upper, partner, stacked), jnp.where(upper, stacked, partner)], axis=1
                )
                rhs = folded[0]
                faces = tuple((folded[place] for place in range(1, 7)))
        level = assemble(faces, group)
        field = line_solve(level, rhs)
        residual = neighbour_terms(level, field)
        levels.append(level)
        fields.append(field)
        sources.append(rhs)
    face_x, low_x, face_y, low_y, face_z, shift = faces
    coarse = jnp.stack(
        [
            coarse_face(face_x, 1, 1),
            coarse_face(face_y, 0, 1),
            coarse_face(face_z, 2, 1),
            0.25 * coarse_sum(shift),
        ]
    )
    whole = gather_whole(coarse, WHOLE_FROM)
    whole_rhs = gather_whole((0.25 * coarse_sum(residual))[None], WHOLE_FROM)[0]
    face_x, face_y, face_z, shift = (whole[0], whole[1], whole[2], whole[3])
    chain = [whole_level(face_x, face_y, face_z, shift)]
    for depth in range(WHOLE_FROM + 1, LEVELS):
        face_x = coarse_face(face_x, 1, 1)
        face_y = coarse_face(face_y, 0, 1)
        face_z = coarse_face(face_z, 2, 1)
        shift = 0.25 * coarse_sum(shift)
        chain.append(whole_level(face_x, face_y, face_z, shift))
    whole_correction = whole_cycle(chain, 0, whole_rhs)
    rows, width, height = coarse.shape[1:]
    spread = 2 ** max(WHOLE_FROM - 2, 0)
    correction = lax.dynamic_slice(
        whole_correction,
        (rows * (lax.axis_index(GY) // spread), width * lax.axis_index("gx"), 0),
        (rows, width, height),
    )
    for depth in range(WHOLE_FROM - 1, -1, -1):
        if depth < WHOLE_FROM - 1 and depth + 1 >= 2:
            half = correction.shape[0] // 2
            correction = lax.dynamic_slice_in_dim(correction, upper_flag(depth - 1) * half, half, 0)
        field = fields[depth] + prolong(correction)
        correction = relax(levels[depth], field, sources[depth])
    return correction


def solution(mesh):
    finer = Mesh(mesh.devices.reshape(mesh.shape["gx"], 8, 4, 2), ("gx", "gy_0", "gy_1", "gy_2"))
    return jax.shard_map(
        body,
        mesh=finer,
        in_specs=(
            P(GY, "gx", None),
            P(GY, "gx", None),
            P(GY, "gx", None),
            P(GY, "gx", None),
            P(GY, "gx", None),
        ),
        out_specs=P(GY, "gx", None),
        check_vma=False,
    )
```

profile of v0, /device:TPU:57, one launch (start us, length us, event | category | flops | bytes accessed | tf_op | source)
XLA Modules:
  0.0 2341.1 jit_solution(15719183095452096029)
XLA Ops:
  2.1 3.7 collective-permute-start.3
  7.1 4.0 collective-permute-start
  13.1 9.7 reshape.649
  22.9 4.7 reduce_sum.270
  29.2 2.4 slice.7159
  33.6 3.5 all_to_all.86
  39.6 14.6 all-to-all-start.1
  72.9 10.7 all-to-all-start.2
  83.7 9.4 all-to-all-done.2
  95.1 3.0 collective-permute-start.4
  99.5 2.9 collective-permute-done.5
  102.6 9.7 reshape.648
  112.3 4.0 reduce_sum.268
  118.2 5.5 all_to_all.87
  125.5 4.0 all-to-all-start.4
  130.4 7.9 all-to-all-done.4
  144.6 5.4 all-to-all-start.5
  151.3 8.8 all-to-all-done.5
  160.6 3.5 collective-permute-start.6
  165.5 3.2 collective-permute-done.7
  170.2 3.5 collective-permute-start.8
  176.4 514.1 %all-gather.1 = f32[1024,2,4,16]{3,2,1,0:T(4,128)S(1)} all-gather(f32[4,2,4,16]{3,2,1,0:T(4,128)S(1)} %pad_maximum_fusion.47), channel_id=3, replica_groups=mesh['gx'=8,'gy_0'=8,'gy_1'=4,'gy_2'=2] {'gx','gy_0','gy_1'}, dimensions={0}, use_global_device_ids=true | all-gather | bytes 526336 | tf_op jit(solution)/shard_map/all_gather | solution.py:287
  691.8 3.0 slice_reduce_fusion.8
  716.5 187.0 %all-to-all-start.6 = ((f32[64,6,1,256]{3,2,1,0:T(1,128)}), f32[64,6,1,256]{3,2,1,0:T(1,128)}, u32[]{:S(2)}, u32[]{:S(2)}) async-start(f32[64,6,1,256]{3,2,1,0:T(1,128)} %broadcast_in_dim.193), calls=%async_computation.6 | async-start | bytes 786432 | tf_op jit(solution)/shard_map/all_to_all | solution.py:40
  903.4 2.1 copy.1201
  913.3 2.1 slice.7908
  915.4 2.1 copy.1198
  917.5 2.1 copy.1199
  932.1 5.1 slice.7913
  937.2 2.3 copy.1206
  945.7 2.1 broadcast_multiply_fusion.3
  956.0 2.5 mul.28970
  964.7 3.7 add_add_fusion.1
  1296.1 3.0 collective-permute-done.10
  1304.6 503.7 %all-gather = f32[512,4,16]{2,1,0:T(4,128)S(1)} all-gather(f32[2,4,16]{2,1,0:T(4,128)S(1)} %broadcast_multiply_fusion.16), channel_id=2, replica_groups=mesh['gx'=8,'gy_0'=8,'gy_1'=4,'gy_2'=2] {'gx','gy_0','gy_1'}, dimensions={0}, use_global_device_ids=true | all-gather | bytes 131584 | tf_op jit(solution)/shard_map/all_gather | solution.py:287
  1808.6 2.0 subtract_divide_fusion.73
  1817.6 2.3 constant_dynamic-update-slice_fusion.111
  1835.1 2.1 multiply_add_fusion
  1837.1 2.5 copy.1196
  1839.6 11.0 reshape.658
  1850.6 4.7 reduce_sum.287
  1858.6 2.3 constant_dynamic-update-slice_fusion.144
  1865.9 2.4 reshape.659
  1895.4 2.7 copy.1224
  1904.1 2.5 multiply_subtract_fusion.25
  1948.7 2.5 fusion.469
  1980.1 2.0 fusion.155
  1996.3 10.9 stack.311
  2008.4 3.6 collective-permute-start.11
  2013.4 3.0 collective-permute-done.12
  2020.7 185.1 %all-to-all-start.7 = ((f32[64,6,1,256]{3,2,1,0:T(1,128)}), f32[64,6,1,256]{3,2,1,0:T(1,128)S(1)}, u32[]{:S(2)}, u32[]{:S(2)}) async-start(f32[64,6,1,256]{3,2,1,0:T(1,128)} %broadcast_in_dim.222), calls=%async_computation.7 | async-start | bytes 786432 | tf_op jit(solution)/shard_map/all_to_all | solution.py:40
  2206.5 14.5 all-to-all-done.7
  2226.8 10.4 collective-permute-start.13
  2238.7 3.1 collective-permute-done.14
  2242.7 4.8 all_to_all.88
  2248.6 13.2 all_to_all.89
  2267.7 15.1 all_to_all.90
  2285.1 3.6 collective-permute-start.15
  2290.1 2.9 collective-permute-done.16
  2295.3 5.3 all_to_all.91
  2302.6 4.1 all-to-all-start.12
  2306.7 9.1 all-to-all-done.12
  2322.3 5.8 all-to-all-start.13
  2328.2 9.5 all-to-all-done.13
  (2745 shorter events, 629.3 us)
Async XLA Ops:
  2.1 25.4 %collective-permute-start.3 = (f32[3,1,32,128]{3,2,1,0:T(8,128)S(1)}, f32[3,1,32,128]{3,2,1,0:T(8,128)S(1)}, u32[]{:S(2)}, u32[]{:S(2)}) collective-permute-start(f32[3,1,32,128]{3,2,1,0:T(8,128)S(1)} %get-tuple-element.941), channel_id=1, source_target_pairs={{0,1},{1,2},{2,3},{3,4},{4,5},{5,6},{6,7},{7,8},{8,9},{9,10},{10,1... | collective-permute-start | bytes 147464 | tf_op jit(solution)/shard_map/ppermute | solution.py:73
  5.8 21.7 collective-permute-start.1
  7.1 20.4 collective-permute-start
  11.1 17.2 collective-permute-start.2
  27.6 66.4 %copy-start.22 = (f32[8,32,128]{2,1,0:T(8,128)}, f32[8,32,128]{2,1,0:T(8,128)S(1)}, u32[]{:S(2)}) copy-start(f32[8,32,128]{2,1,0:T(8,128)S(1)} %get-tuple-element.904) | copy-start | bytes 393220
  28.5 65.7 %copy-start.23 = (f32[8,32,128]{2,1,0:T(8,128)}, f32[8,32,128]{2,1,0:T(8,128)S(1)}, u32[]{:S(2)}) copy-start(f32[8,32,128]{2,1,0:T(8,128)S(1)} %get-tuple-element.908) | copy-start | bytes 393220
  28.5 74.0 %copy-start.15 = (f32[8,32,128]{2,1,0:T(8,128)}, f32[8,32,128]{2,1,0:T(8,128)S(1)}, u32[]{:S(2)}) copy-start(f32[8,32,128]{2,1,0:T(8,128)S(1)} %get-tuple-element.906) | copy-start | bytes 393220
  28.5 74.0 %copy-start.17 = (f32[8,32,128]{2,1,0:T(8,128)}, f32[8,32,128]{2,1,0:T(8,128)S(1)}, u32[]{:S(2)}) copy-start(f32[8,32,128]{2,1,0:T(8,128)S(1)} %get-tuple-element.907) | copy-start | bytes 393220
  39.6 25.8 %all-to-all-start.1 = ((f32[32,1,768]{2,1,0:T(1,128)}), f32[32,1,768]{2,1,0:T(1,128)}, u32[]{:S(2)}, u32[]{:S(2)}) async-start(f32[32,1,768]{2,1,0:T(1,128)} %reshape.749), calls=%async_computation.1 | async-start | bytes 196608 | tf_op jit(solution)/shard_map/all_to_all | solution.py:28
  56.0 112.8 %copy-start.56 = (f32[4,16,64]{2,1,0:T(8,128)}, f32[4,16,64]{2,1,0:T(8,128)S(1)}, u32[]{:S(2)}) copy-start(f32[4,16,64]{2,1,0:T(8,128)S(1)} %broadcast_reduce_fusion.7) | copy-start | bytes 49156
  60.2 108.6 %copy-start.29 = (f32[4,16,64]{2,1,0:T(8,128)}, f32[4,16,64]{2,1,0:T(8,128)S(1)}, u32[]{:S(2)}) copy-start(f32[4,16,64]{2,1,0:T(8,128)S(1)} %get-tuple-element.1473) | copy-start | bytes 49156
  60.2 108.6 %copy-start.31 = (f32[4,16,64]{2,1,0:T(8,128)}, f32[4,16,64]{2,1,0:T(8,128)S(1)}, u32[]{:S(2)}) copy-start(f32[4,16,64]{2,1,0:T(8,128)S(1)} %broadcast_multiply_fusion.9) | copy-start | bytes 49156
  63.7 105.1 %copy-start.58 = (f32[4,16,64]{2,1,0:T(8,128)}, f32[4,16,64]{2,1,0:T(8,128)S(1)}, u32[]{:S(2)}) copy-start(f32[4,16,64]{2,1,0:T(8,128)S(1)} %get-tuple-element.1476) | copy-start | bytes 49156
  63.8 53.1 %copy-start.60 = (f32[4,16,64]{2,1,0:T(8,128)}, f32[4,16,64]{2,1,0:T(8,128)S(1)}, u32[]{:S(2)}) copy-start(f32[4,16,64]{2,1,0:T(8,128)S(1)} %get-tuple-element.1147) | copy-start | bytes 49156
  63.8 53.1 %copy-start.110 = (f32[4,16,64]{2,1,0:T(8,128)}, f32[4,16,64]{2,1,0:T(8,128)S(1)}, u32[]{:S(2)}) copy-start(f32[4,16,64]{2,1,0:T(8,128)S(1)} %get-tuple-element.1142) | copy-start | bytes 49156
  63.9 96.5 %copy-start.144 = (f32[4,16,64]{2,1,0:T(8,128)}, f32[4,16,64]{2,1,0:T(8,128)S(1)}, u32[]{:S(2)}) copy-start(f32[4,16,64]{2,1,0:T(8,128)S(1)} %get-tuple-element.1145) | copy-start | bytes 49156
  63.9 96.6 %copy-start.143 = (f32[4,16,64]{2,1,0:T(8,128)}, f32[4,16,64]{2,1,0:T(8,128)S(1)}, u32[]{:S(2)}) copy-start(f32[4,16,64]{2,1,0:T(8,128)S(1)} %get-tuple-element.1148) | copy-start | bytes 49156
  64.0 52.4 %copy-start.188 = (f32[1,16,64]{2,1,0:T(8,128)}, f32[1,16,64]{2,1,0:T(8,128)S(1)}, u32[]{:S(2)}) copy-start(f32[1,16,64]{2,1,0:T(8,128)S(1)} %get-tuple-element.818) | copy-start | bytes 12292
  64.0 52.6 %copy-start.156 = (f32[1,16,64]{2,1,0:T(8,128)}, f32[1,16,64]{2,1,0:T(8,128)S(1)}, u32[]{:S(2)}) copy-start(f32[1,16,64]{2,1,0:T(8,128)S(1)} %get-tuple-element.814) | copy-start | bytes 12292
  64.0 53.0 %copy-start.158 = (f32[1,16,64]{2,1,0:T(8,128)}, f32[1,16,64]{2,1,0:T(8,128)S(1)}, u32[]{:S(2)}) copy-start(f32[1,16,64]{2,1,0:T(8,128)S(1)} %get-tuple-element.815) | copy-start | bytes 12292
  64.0 53.0 %copy-start.160 = (f32[1,16,64]{2,1,0:T(8,128)}, f32[1,16,64]{2,1,0:T(8,128)S(1)}, u32[]{:S(2)}) copy-start(f32[1,16,64]{2,1,0:T(8,128)S(1)} %get-tuple-element.817) | copy-start | bytes 12292
  64.0 53.0 %copy-start.162 = (f32[1,16,64]{2,1,0:T(8,128)}, f32[1,16,64]{2,1,0:T(8,128)S(1)}, u32[]{:S(2)}) copy-start(f32[1,16,64]{2,1,0:T(8,128)S(1)} %get-tuple-element.819) | copy-start | bytes 12292
  64.0 53.0 %copy-start.169 = (f32[1,16,64]{2,1,0:T(8,128)}, f32[1,16,64]{2,1,0:T(8,128)S(1)}, u32[]{:S(2)}) copy-start(f32[1,16,64]{2,1,0:T(8,128)S(1)} %get-tuple-element.816) | copy-start | bytes 12292
  64.0 96.5 %copy-start.139 = (f32[1,16,64]{2,1,0:T(8,128)}, f32[1,16,64]{2,1,0:T(8,128)S(1)}, u32[]{:S(2)}) copy-start(f32[1,16,64]{2,1,0:T(8,128)S(1)} %get-tuple-element.812) | copy-start | bytes 12292
  72.9 20.1 all-to-all-start.2
  95.1 4.4 collective-permute-start.4
  98.1 4.4 collective-permute-start.5
  116.4 44.1 %copy-start.141 = (f32[1,16,64]{2,1,0:T(8,128)}, f32[1,16,64]{2,1,0:T(8,128)S(1)}, u32[]{:S(2)}) copy-start(f32[1,16,64]{2,1,0:T(8,128)S(1)} %get-tuple-element.821) | copy-start | bytes 12292
  116.6 43.9 %copy-start.164 = (f32[1,16,64]{2,1,0:T(8,128)}, f32[1,16,64]{2,1,0:T(8,128)S(1)}, u32[]{:S(2)}) copy-start(f32[1,16,64]{2,1,0:T(8,128)S(1)} %get-tuple-element.831) | copy-start | bytes 12292
  116.6 43.9 %copy-start.166 = (f32[1,16,64]{2,1,0:T(8,128)}, f32[1,16,64]{2,1,0:T(8,128)S(1)}, u32[]{:S(2)}) copy-start(f32[1,16,64]{2,1,0:T(8,128)S(1)} %get-tuple-element.834) | copy-start | bytes 12292
  116.6 43.9 %copy-start.184 = (f32[1,16,64]{2,1,0:T(8,128)}, f32[1,16,64]{2,1,0:T(8,128)S(1)}, u32[]{:S(2)}) copy-start(f32[1,16,64]{2,1,0:T(8,128)S(1)} %get-tuple-element.832) | copy-start | bytes 12292
  116.6 43.9 %copy-start.186 = (f32[1,16,64]{2,1,0:T(8,128)}, f32[1,16,64]{2,1,0:T(8,128)S(1)}, u32[]{:S(2)}) copy-start(f32[1,16,64]{2,1,0:T(8,128)S(1)} %get-tuple-element.833) | copy-start | bytes 12292
  117.0 43.5 %copy-start.171 = (f32[1,16,64]{2,1,0:T(8,128)}, f32[1,16,64]{2,1,0:T(8,128)S(1)}, u32[]{:S(2)}) copy-start(f32[1,16,64]{2,1,0:T(8,128)S(1)} %get-tuple-element.828) | copy-start | bytes 12292
  117.0 43.5 %copy-start.173 = (f32[1,16,64]{2,1,0:T(8,128)}, f32[1,16,64]{2,1,0:T(8,128)S(1)}, u32[]{:S(2)}) copy-start(f32[1,16,64]{2,1,0:T(8,128)S(1)} %get-tuple-element.829) | copy-start | bytes 12292
  117.0 43.5 %copy-start.175 = (f32[1,16,64]{2,1,0:T(8,128)}, f32[1,16,64]{2,1,0:T(8,128)S(1)}, u32[]{:S(2)}) copy-start(f32[1,16,64]{2,1,0:T(8,128)S(1)} %get-tuple-element.830) | copy-start | bytes 12292
  117.0 43.5 %copy-start.177 = (f32[1,16,64]{2,1,0:T(8,128)}, f32[1,16,64]{2,1,0:T(8,128)S(1)}, u32[]{:S(2)}) copy-start(f32[1,16,64]{2,1,0:T(8,128)S(1)} %get-tuple-element.1030) | copy-start | bytes 12292
  117.0 43.5 %copy-start.179 = (f32[1,16,64]{2,1,0:T(8,128)}, f32[1,16,64]{2,1,0:T(8,128)S(1)}, u32[]{:S(2)}) copy-start(f32[1,16,64]{2,1,0:T(8,128)S(1)} %get-tuple-element.1031) | copy-start | bytes 12292
  117.0 43.5 %copy-start.181 = (f32[1,16,64]{2,1,0:T(8,128)}, f32[1,16,64]{2,1,0:T(8,128)S(1)}, u32[]{:S(2)}) copy-start(f32[1,16,64]{2,1,0:T(8,128)S(1)} %get-tuple-element.1032) | copy-start | bytes 12292
  125.5 12.7 all-to-all-start.4
  144.6 15.5 all-to-all-start.5
  160.4 530.1 %copy-start.190 = (f32[16,64]{1,0:T(8,128)}, f32[16,64]{1,0:T(8,128)S(1)}, u32[]{:S(2)}) copy-start(f32[16,64]{1,0:T(8,128)S(1)} %multiply_bitcast_fusion.7) | copy-start | bytes 12292
  160.5 530.1 %copy-start.192 = (f32[16,64]{1,0:T(8,128)}, f32[16,64]{1,0:T(8,128)S(1)}, u32[]{:S(2)}) copy-start(f32[16,64]{1,0:T(8,128)S(1)} %multiply_bitcast_fusion.6) | copy-start | bytes 12292
  160.6 4.9 collective-permute-start.6
  164.2 4.6 collective-permute-start.7
  170.2 4.3 collective-permute-start.8
  174.6 517.2 %copy-start.11 = (f32[7,2,8,32]{3,2,1,0:T(8,128)}, f32[7,2,8,32]{3,2,1,0:T(8,128)S(1)}, u32[]{:S(2)}) copy-start(f32[7,2,8,32]{3,2,1,0:T(8,128)S(1)} %get-tuple-element.1013) | copy-start | bytes 43012
  174.6 517.2 %copy-start.13 = (f32[7,2,8,32]{3,2,1,0:T(8,128)}, f32[7,2,8,32]{3,2,1,0:T(8,128)S(1)}, u32[]{:S(2)}) copy-start(f32[7,2,8,32]{3,2,1,0:T(8,128)S(1)} %get-tuple-element.1014) | copy-start | bytes 43012
  174.6 517.2 %copy-start.25 = (f32[4,8,32]{2,1,0:T(8,128)}, f32[4,8,32]{2,1,0:T(8,128)S(1)}, u32[]{:S(2)}) copy-start(f32[4,8,32]{2,1,0:T(8,128)S(1)} %fusion.81) | copy-start | bytes 12292
  174.8 533.3 %copy-start.129 = (f32[4,8,32]{2,1,0:T(8,128)}, f32[4,8,32]{2,1,0:T(8,128)S(1)}, u32[]{:S(2)}) copy-start(f32[4,8,32]{2,1,0:T(8,128)S(1)} %get-tuple-element.1012) | copy-start | bytes 12292
  174.8 533.3 %copy-start.147 = (f32[4,8,32]{2,1,0:T(8,128)}, f32[4,8,32]{2,1,0:T(8,128)S(1)}, u32[]{:S(2)}) copy-start(f32[4,8,32]{2,1,0:T(8,128)S(1)} %get-tuple-element.787) | copy-start | bytes 12292
  716.5 252.0 %all-to-all-start.6 = ((f32[64,6,1,256]{3,2,1,0:T(1,128)}), f32[64,6,1,256]{3,2,1,0:T(1,128)}, u32[]{:S(2)}, u32[]{:S(2)}) async-start(f32[64,6,1,256]{3,2,1,0:T(1,128)} %broadcast_in_dim.193), calls=%async_computation.6 | async-start | bytes 786432 | tf_op jit(solution)/shard_map/all_to_all | solution.py:40
  1293.5 2.7 collective-permute-start.9
  1294.8 4.3 collective-permute-start.10
  1303.8 506.8 %copy-start = (f32[64,32,16]{2,1,0:T(8,128)S(1)}, f32[64,32,16]{2,1,0:T(8,128)}, u32[]{:S(2)}) copy-start(f32[64,32,16]{2,1,0:T(8,128)} %get-tuple-element.923) | copy-start | bytes 393220
  1303.8 506.8 %copy-start.7 = (f32[64,32,16]{2,1,0:T(8,128)S(1)}, f32[64,32,16]{2,1,0:T(8,128)}, u32[]{:S(2)}) copy-start(f32[64,32,16]{2,1,0:T(8,128)} %get-tuple-element.922) | copy-start | bytes 393220
  2008.4 5.0 collective-permute-start.11
  2012.0 4.3 collective-permute-start.12
  2020.7 200.2 %all-to-all-start.7 = ((f32[64,6,1,256]{3,2,1,0:T(1,128)}), f32[64,6,1,256]{3,2,1,0:T(1,128)S(1)}, u32[]{:S(2)}, u32[]{:S(2)}) async-start(f32[64,6,1,256]{3,2,1,0:T(1,128)} %broadcast_in_dim.222), calls=%async_computation.7 | async-start | bytes 786432 | tf_op jit(solution)/shard_map/all_to_all | solution.py:40
  2226.8 11.9 collective-permute-start.13
  2237.1 4.6 collective-permute-start.14
  2285.1 5.0 collective-permute-start.15
  2288.7 4.4 collective-permute-start.16
  2302.6 13.2 all-to-all-start.12
  2322.3 15.3 all-to-all-start.13
  (200 other events, 2103.3 us)
where the time goes:
time: 2370 us; the launch traced here: 2340 us
  blocking collectives  1070 us (45%)
  local copies, waits for them, and re-layouts  494 us (21%)
  starting transfers between devices  464 us (20%)
  other arithmetic  229 us (10%)
  waiting for transfers between devices  78.1 us (3%)
    all_gather x2, blocking collectives, gather_whole(): parts = lax.all_gather(block, axes, axis=0)  1020 us
    all_to_all x2, starting transfers between devices, copy_for_each(): lax.all_to_all(jnp.broadcast_to(x[None], (count, *x.shape)), axis, 0, 0,...  372 us
    slice x706, local copies, waits for them, and re-layouts, reduced_local(): inclusive = lax.associative_scan(chain_forward, terms, axis=0)  139 us
  transfers between devices with their start and end apart: 25, of which 13 were waited for; matrix products, arithmetic and copies ran while one was open for 4% of the time, Pallas kernels for 0%

commit v1 on v0

--- a/solution.py
+++ b/solution.py
@@ -239,8 +239,14 @@
         prev_last, next_first = reduced_local(
             moved[0], moved[1], moved[2], moved[3], moved[4], moved[5]
         )
-        back = lax.all_to_all(
-            jnp.stack([prev_last, next_first]), GY, split_axis=1, concat_axis=2, tiled=True
+        back = jnp.concatenate(
+            lax.all_to_all(
+                jnp.stack(jnp.split(jnp.stack([prev_last, next_first]), lax.axis_size(GY), axis=1)),
+                GY,
+                0,
+                0,
+            ),
+            axis=2,
         )
         return (back[0, 0].reshape(shape), back[1, 0].reshape(shape))
     whole = gather_directly(packed, GY, 1)

time: 2370 us -> 2410 us (1.017)
  local copies, waits for them, and re-layouts: 494 us -> 532 us
    unnamed x637 -> x889, local copies, waits for them, and re-layouts: 30.6 us -> 68.2 us
where the time goes in v1:
time: 2410 us; the launch traced here: 2380 us
  blocking collectives  1060 us (44%)
  local copies, waits for them, and re-layouts  532 us (22%)
  starting transfers between devices  465 us (19%)
  other arithmetic  233 us (10%)
  waiting for transfers between devices  78.4 us (3%)
    all_gather x2, blocking collectives, gather_whole(): parts = lax.all_gather(block, axes, axis=0)  1020 us
    all_to_all x2, starting transfers between devices, copy_for_each(): lax.all_to_all(jnp.broadcast_to(x[None], (count, *x.shape)), axis, 0, 0,...  372 us
    slice x706, local copies, waits for them, and re-layouts, reduced_local(): inclusive = lax.associative_scan(chain_forward, terms, axis=0)  139 us
    unnamed x889, local copies, waits for them, and re-layouts  68.2 us
  transfers between devices with their start and end apart: 25, of which 13 were waited for; matrix products, arithmetic and copies ran while one was open for 4% of the time, Pallas kernels for 0%

profile of v1, /device:TPU:57, one launch (start us, length us, event | category | flops | bytes accessed | tf_op | source)
XLA Modules:
  0.0 2383.4 jit_solution(12927642531898436762)
XLA Ops:
  2.1 3.7 collective-permute-start.3
  7.1 4.0 collective-permute-start
  13.1 9.8 reshape.646
  23.0 4.7 reduce_sum.270
  29.3 2.4 slice.7155
  33.7 3.5 all_to_all.70
  39.9 14.6 all-to-all-start.1
  74.1 10.7 all-to-all-start.2
  84.8 9.4 all-to-all-done.2
  96.4 3.0 collective-permute-start.4
  100.8 2.9 collective-permute-done.5
  103.9 9.8 reshape.645
  113.7 4.0 reduce_sum.268
  119.6 5.5 all_to_all.71
  127.0 4.0 all-to-all-start.4
  131.9 7.8 all-to-all-done.4
  183.8 5.5 all-to-all-start.5
  190.5 8.8 all-to-all-done.5
  199.9 3.5 collective-permute-start.6
  204.8 3.2 collective-permute-done.7
  209.5 3.5 collective-permute-start.8
  215.6 514.1 %all-gather.1 = f32[1024,2,4,16]{3,2,1,0:T(4,128)S(1)} all-gather(f32[4,2,4,16]{3,2,1,0:T(4,128)S(1)} %pad_maximum_fusion.45), channel_id=3, replica_groups=mesh['gx'=8,'gy_0'=8,'gy_1'=4,'gy_2'=2] {'gx','gy_0','gy_1'}, dimensions={0}, use_global_device_ids=true | all-gather | bytes 526336 | tf_op jit(solution)/shard_map/all_gather | solution.py:293
  730.9 3.0 slice_reduce_fusion.8
  755.7 187.6 %all-to-all-start.6 = ((f32[64,6,1,256]{3,2,1,0:T(1,128)}), f32[64,6,1,256]{3,2,1,0:T(1,128)}, u32[]{:S(2)}, u32[]{:S(2)}) async-start(f32[64,6,1,256]{3,2,1,0:T(1,128)} %broadcast_in_dim.193), calls=%async_computation.6 | async-start | bytes 786432 | tf_op jit(solution)/shard_map/all_to_all | solution.py:40
  943.3 2.0 copy.1585
  953.1 2.1 slice.7904
  955.2 2.0 copy.1582
  957.2 2.1 copy.1583
  971.8 5.1 slice.7909
  976.9 2.3 copy.1590
  985.5 2.1 broadcast_multiply_fusion.3
  995.7 2.4 mul.28970
  1004.4 3.8 add_add_fusion.1
  1334.9 3.0 collective-permute-done.10
  1343.4 503.3 %all-gather = f32[512,4,16]{2,1,0:T(4,128)S(1)} all-gather(f32[2,4,16]{2,1,0:T(4,128)S(1)} %broadcast_multiply_fusion.16), channel_id=2, replica_groups=mesh['gx'=8,'gy_0'=8,'gy_1'=4,'gy_2'=2] {'gx','gy_0','gy_1'}, dimensions={0}, use_global_device_ids=true | all-gather | bytes 131584 | tf_op jit(solution)/shard_map/all_gather | solution.py:293
  1847.0 2.0 subtract_divide_fusion.73
  1855.9 2.3 constant_dynamic-update-slice_fusion.239
  1873.4 2.1 multiply_add_fusion
  1875.5 2.5 copy.1580
  1877.9 11.1 reshape.656
  1889.0 4.7 reduce_sum.287
  1897.0 2.3 constant_dynamic-update-slice_fusion.272
  1904.3 2.4 reshape.657
  1933.9 2.7 copy.1608
  1942.6 2.5 multiply_subtract_fusion.25
  1987.0 2.5 fusion.849
  2018.3 2.0 fusion.409
  2034.5 10.9 stack.1586
  2046.6 3.6 collective-permute-start.11
  2051.6 3.0 collective-permute-done.12
  2058.9 184.8 %all-to-all-start.7 = ((f32[64,6,1,256]{3,2,1,0:T(1,128)}), f32[64,6,1,256]{3,2,1,0:T(1,128)S(1)}, u32[]{:S(2)}, u32[]{:S(2)}) async-start(f32[64,6,1,256]{3,2,1,0:T(1,128)} %broadcast_in_dim.222), calls=%async_computation.7 | async-start | bytes 786432 | tf_op jit(solution)/shard_map/all_to_all | solution.py:40
  2244.5 14.5 all-to-all-done.7
  2264.7 10.6 collective-permute-start.13
  2276.9 3.1 collective-permute-done.14
  2280.9 4.8 all_to_all.72
  2286.9 13.2 all_to_all.73
  2308.8 15.1 all_to_all.74
  2326.1 3.6 collective-permute-start.15
  2331.2 2.9 collective-permute-done.16
  2336.3 5.3 all_to_all.75
  2343.8 4.1 all-to-all-start.12
  2347.9 9.4 all-to-all-done.12
  2364.8 5.4 all-to-all-start.13
  2370.3 9.5 all-to-all-done.13
  (3031 shorter events, 670.4 us)
Async XLA Ops:
  2.1 25.5 %collective-permute-start.3 = (f32[3,1,32,128]{3,2,1,0:T(8,128)S(1)}, f32[3,1,32,128]{3,2,1,0:T(8,128)S(1)}, u32[]{:S(2)}, u32[]{:S(2)}) collective-permute-start(f32[3,1,32,128]{3,2,1,0:T(8,128)S(1)} %get-tuple-element.1067), channel_id=1, source_target_pairs={{0,1},{1,2},{2,3},{3,4},{4,5},{5,6},{6,7},{7,8},{8,9},{9,10},{10,1... | collective-permute-start | bytes 147464 | tf_op jit(solution)/shard_map/ppermute | solution.py:73
  5.8 21.8 collective-permute-start.1
  7.1 20.5 collective-permute-start
  11.1 17.3 collective-permute-start.2
  27.7 67.7 %copy-start.22 = (f32[8,32,128]{2,1,0:T(8,128)}, f32[8,32,128]{2,1,0:T(8,128)S(1)}, u32[]{:S(2)}) copy-start(f32[8,32,128]{2,1,0:T(8,128)S(1)} %get-tuple-element.1030) | copy-start | bytes 393220
  28.5 66.9 %copy-start.23 = (f32[8,32,128]{2,1,0:T(8,128)}, f32[8,32,128]{2,1,0:T(8,128)S(1)}, u32[]{:S(2)}) copy-start(f32[8,32,128]{2,1,0:T(8,128)S(1)} %get-tuple-element.1034) | copy-start | bytes 393220
  28.6 75.2 %copy-start.15 = (f32[8,32,128]{2,1,0:T(8,128)}, f32[8,32,128]{2,1,0:T(8,128)S(1)}, u32[]{:S(2)}) copy-start(f32[8,32,128]{2,1,0:T(8,128)S(1)} %get-tuple-element.1032) | copy-start | bytes 393220
  28.6 75.2 %copy-start.17 = (f32[8,32,128]{2,1,0:T(8,128)}, f32[8,32,128]{2,1,0:T(8,128)S(1)}, u32[]{:S(2)}) copy-start(f32[8,32,128]{2,1,0:T(8,128)S(1)} %get-tuple-element.1033) | copy-start | bytes 393220
  39.9 25.8 %all-to-all-start.1 = ((f32[32,1,768]{2,1,0:T(1,128)}), f32[32,1,768]{2,1,0:T(1,128)}, u32[]{:S(2)}, u32[]{:S(2)}) async-start(f32[32,1,768]{2,1,0:T(1,128)} %reshape.877), calls=%async_computation.1 | async-start | bytes 196608 | tf_op jit(solution)/shard_map/all_to_all | solution.py:28
  56.3 151.8 %copy-start.56 = (f32[4,16,64]{2,1,0:T(8,128)}, f32[4,16,64]{2,1,0:T(8,128)S(1)}, u32[]{:S(2)}) copy-start(f32[4,16,64]{2,1,0:T(8,128)S(1)} %broadcast_reduce_fusion.7) | copy-start | bytes 49156
  60.4 147.6 %copy-start.29 = (f32[4,16,64]{2,1,0:T(8,128)}, f32[4,16,64]{2,1,0:T(8,128)S(1)}, u32[]{:S(2)}) copy-start(f32[4,16,64]{2,1,0:T(8,128)S(1)} %get-tuple-element.1725) | copy-start | bytes 49156
  60.4 147.6 %copy-start.31 = (f32[4,16,64]{2,1,0:T(8,128)}, f32[4,16,64]{2,1,0:T(8,128)S(1)}, u32[]{:S(2)}) copy-start(f32[4,16,64]{2,1,0:T(8,128)S(1)} %broadcast_multiply_fusion.9) | copy-start | bytes 49156
  64.0 144.1 %copy-start.58 = (f32[4,16,64]{2,1,0:T(8,128)}, f32[4,16,64]{2,1,0:T(8,128)S(1)}, u32[]{:S(2)}) copy-start(f32[4,16,64]{2,1,0:T(8,128)S(1)} %get-tuple-element.1728) | copy-start | bytes 49156
  64.1 54.2 %copy-start.60 = (f32[4,16,64]{2,1,0:T(8,128)}, f32[4,16,64]{2,1,0:T(8,128)S(1)}, u32[]{:S(2)}) copy-start(f32[4,16,64]{2,1,0:T(8,128)S(1)} %get-tuple-element.1399) | copy-start | bytes 49156
  64.1 54.2 %copy-start.110 = (f32[4,16,64]{2,1,0:T(8,128)}, f32[4,16,64]{2,1,0:T(8,128)S(1)}, u32[]{:S(2)}) copy-start(f32[4,16,64]{2,1,0:T(8,128)S(1)} %get-tuple-element.1394) | copy-start | bytes 49156
  64.1 135.5 %copy-start.144 = (f32[4,16,64]{2,1,0:T(8,128)}, f32[4,16,64]{2,1,0:T(8,128)S(1)}, u32[]{:S(2)}) copy-start(f32[4,16,64]{2,1,0:T(8,128)S(1)} %get-tuple-element.1397) | copy-start | bytes 49156
  64.1 135.6 %copy-start.143 = (f32[4,16,64]{2,1,0:T(8,128)}, f32[4,16,64]{2,1,0:T(8,128)S(1)}, u32[]{:S(2)}) copy-start(f32[4,16,64]{2,1,0:T(8,128)S(1)} %get-tuple-element.1400) | copy-start | bytes 49156
  64.2 53.8 %copy-start.156 = (f32[1,16,64]{2,1,0:T(8,128)}, f32[1,16,64]{2,1,0:T(8,128)S(1)}, u32[]{:S(2)}) copy-start(f32[1,16,64]{2,1,0:T(8,128)S(1)} %get-tuple-element.940) | copy-start | bytes 12292
  64.2 54.1 %copy-start.158 = (f32[1,16,64]{2,1,0:T(8,128)}, f32[1,16,64]{2,1,0:T(8,128)S(1)}, u32[]{:S(2)}) copy-start(f32[1,16,64]{2,1,0:T(8,128)S(1)} %get-tuple-element.941) | copy-start | bytes 12292
  64.2 54.1 %copy-start.160 = (f32[1,16,64]{2,1,0:T(8,128)}, f32[1,16,64]{2,1,0:T(8,128)S(1)}, u32[]{:S(2)}) copy-start(f32[1,16,64]{2,1,0:T(8,128)S(1)} %get-tuple-element.943) | copy-start | bytes 12292
  64.2 54.1 %copy-start.162 = (f32[1,16,64]{2,1,0:T(8,128)}, f32[1,16,64]{2,1,0:T(8,128)S(1)}, u32[]{:S(2)}) copy-start(f32[1,16,64]{2,1,0:T(8,128)S(1)} %get-tuple-element.945) | copy-start | bytes 12292
  64.2 54.1 %copy-start.169 = (f32[1,16,64]{2,1,0:T(8,128)}, f32[1,16,64]{2,1,0:T(8,128)S(1)}, u32[]{:S(2)}) copy-start(f32[1,16,64]{2,1,0:T(8,128)S(1)} %get-tuple-element.942) | copy-start | bytes 12292
  64.2 135.5 %copy-start.139 = (f32[1,16,64]{2,1,0:T(8,128)}, f32[1,16,64]{2,1,0:T(8,128)S(1)}, u32[]{:S(2)}) copy-start(f32[1,16,64]{2,1,0:T(8,128)S(1)} %get-tuple-element.938) | copy-start | bytes 12292
  74.1 20.1 all-to-all-start.2
  96.4 4.4 collective-permute-start.4
  99.4 4.4 collective-permute-start.5
  117.8 81.9 %copy-start.141 = (f32[1,16,64]{2,1,0:T(8,128)}, f32[1,16,64]{2,1,0:T(8,128)S(1)}, u32[]{:S(2)}) copy-start(f32[1,16,64]{2,1,0:T(8,128)S(1)} %get-tuple-element.947) | copy-start | bytes 12292
  118.0 81.7 %copy-start.164 = (f32[1,16,64]{2,1,0:T(8,128)}, f32[1,16,64]{2,1,0:T(8,128)S(1)}, u32[]{:S(2)}) copy-start(f32[1,16,64]{2,1,0:T(8,128)S(1)} %get-tuple-element.957) | copy-start | bytes 12292
  118.0 81.7 %copy-start.166 = (f32[1,16,64]{2,1,0:T(8,128)}, f32[1,16,64]{2,1,0:T(8,128)S(1)}, u32[]{:S(2)}) copy-start(f32[1,16,64]{2,1,0:T(8,128)S(1)} %get-tuple-element.960) | copy-start | bytes 12292
  118.0 81.7 %copy-start.184 = (f32[1,16,64]{2,1,0:T(8,128)}, f32[1,16,64]{2,1,0:T(8,128)S(1)}, u32[]{:S(2)}) copy-start(f32[1,16,64]{2,1,0:T(8,128)S(1)} %get-tuple-element.958) | copy-start | bytes 12292
  118.0 81.7 %copy-start.186 = (f32[1,16,64]{2,1,0:T(8,128)}, f32[1,16,64]{2,1,0:T(8,128)S(1)}, u32[]{:S(2)}) copy-start(f32[1,16,64]{2,1,0:T(8,128)S(1)} %get-tuple-element.959) | copy-start | bytes 12292
  118.4 81.4 %copy-start.171 = (f32[1,16,64]{2,1,0:T(8,128)}, f32[1,16,64]{2,1,0:T(8,128)S(1)}, u32[]{:S(2)}) copy-start(f32[1,16,64]{2,1,0:T(8,128)S(1)} %get-tuple-element.954) | copy-start | bytes 12292
  118.4 81.4 %copy-start.173 = (f32[1,16,64]{2,1,0:T(8,128)}, f32[1,16,64]{2,1,0:T(8,128)S(1)}, u32[]{:S(2)}) copy-start(f32[1,16,64]{2,1,0:T(8,128)S(1)} %get-tuple-element.955) | copy-start | bytes 12292
  118.4 81.4 %copy-start.175 = (f32[1,16,64]{2,1,0:T(8,128)}, f32[1,16,64]{2,1,0:T(8,128)S(1)}, u32[]{:S(2)}) copy-start(f32[1,16,64]{2,1,0:T(8,128)S(1)} %get-tuple-element.956) | copy-start | bytes 12292
  118.4 81.4 %copy-start.177 = (f32[1,16,64]{2,1,0:T(8,128)}, f32[1,16,64]{2,1,0:T(8,128)S(1)}, u32[]{:S(2)}) copy-start(f32[1,16,64]{2,1,0:T(8,128)S(1)} %get-tuple-element.1156) | copy-start | bytes 12292
  118.4 81.4 %copy-start.179 = (f32[1,16,64]{2,1,0:T(8,128)}, f32[1,16,64]{2,1,0:T(8,128)S(1)}, u32[]{:S(2)}) copy-start(f32[1,16,64]{2,1,0:T(8,128)S(1)} %get-tuple-element.1157) | copy-start | bytes 12292
  118.5 81.4 %copy-start.181 = (f32[1,16,64]{2,1,0:T(8,128)}, f32[1,16,64]{2,1,0:T(8,128)S(1)}, u32[]{:S(2)}) copy-start(f32[1,16,64]{2,1,0:T(8,128)S(1)} %get-tuple-element.1158) | copy-start | bytes 12292
  127.0 12.7 all-to-all-start.4
  144.2 65.2 %copy-start.238 = (f32[2,8,32]{2,1,0:T(8,128)S(1)}, f32[2,8,32]{2,1,0:T(8,128)}, u32[]{:S(2)}) copy-start(f32[2,8,32]{2,1,0:T(8,128)} %broadcast_reduce_fusion.11) | copy-start | bytes 6148
  183.8 15.6 all-to-all-start.5
  199.6 530.1 %copy-start.190 = (f32[16,64]{1,0:T(8,128)}, f32[16,64]{1,0:T(8,128)S(1)}, u32[]{:S(2)}) copy-start(f32[16,64]{1,0:T(8,128)S(1)} %multiply_bitcast_fusion.7) | copy-start | bytes 12292
  199.7 530.0 %copy-start.192 = (f32[16,64]{1,0:T(8,128)}, f32[16,64]{1,0:T(8,128)S(1)}, u32[]{:S(2)}) copy-start(f32[16,64]{1,0:T(8,128)S(1)} %multiply_bitcast_fusion.6) | copy-start | bytes 12292
  199.9 4.9 collective-permute-start.6
  203.4 4.6 collective-permute-start.7
  209.5 4.3 collective-permute-start.8
  213.8 517.1 %copy-start.11 = (f32[7,2,8,32]{3,2,1,0:T(8,128)}, f32[7,2,8,32]{3,2,1,0:T(8,128)S(1)}, u32[]{:S(2)}) copy-start(f32[7,2,8,32]{3,2,1,0:T(8,128)S(1)} %get-tuple-element.1139) | copy-start | bytes 43012
  213.8 517.1 %copy-start.13 = (f32[7,2,8,32]{3,2,1,0:T(8,128)}, f32[7,2,8,32]{3,2,1,0:T(8,128)S(1)}, u32[]{:S(2)}) copy-start(f32[7,2,8,32]{3,2,1,0:T(8,128)S(1)} %get-tuple-element.1140) | copy-start | bytes 43012
  213.8 517.1 %copy-start.25 = (f32[4,8,32]{2,1,0:T(8,128)}, f32[4,8,32]{2,1,0:T(8,128)S(1)}, u32[]{:S(2)}) copy-start(f32[4,8,32]{2,1,0:T(8,128)S(1)} %fusion.334) | copy-start | bytes 12292
  214.1 533.2 %copy-start.129 = (f32[4,8,32]{2,1,0:T(8,128)}, f32[4,8,32]{2,1,0:T(8,128)S(1)}, u32[]{:S(2)}) copy-start(f32[4,8,32]{2,1,0:T(8,128)S(1)} %get-tuple-element.1138) | copy-start | bytes 12292
  214.1 533.2 %copy-start.147 = (f32[4,8,32]{2,1,0:T(8,128)}, f32[4,8,32]{2,1,0:T(8,128)S(1)}, u32[]{:S(2)}) copy-start(f32[4,8,32]{2,1,0:T(8,128)S(1)} %get-tuple-element.913) | copy-start | bytes 12292
  755.7 252.5 %all-to-all-start.6 = ((f32[64,6,1,256]{3,2,1,0:T(1,128)}), f32[64,6,1,256]{3,2,1,0:T(1,128)}, u32[]{:S(2)}, u32[]{:S(2)}) async-start(f32[64,6,1,256]{3,2,1,0:T(1,128)} %broadcast_in_dim.193), calls=%async_computation.6 | async-start | bytes 786432 | tf_op jit(solution)/shard_map/all_to_all | solution.py:40
  1332.2 2.7 collective-permute-start.9
  1333.5 4.3 collective-permute-start.10
  1342.5 506.4 %copy-start = (f32[64,32,16]{2,1,0:T(8,128)S(1)}, f32[64,32,16]{2,1,0:T(8,128)}, u32[]{:S(2)}) copy-start(f32[64,32,16]{2,1,0:T(8,128)} %get-tuple-element.1049) | copy-start | bytes 393220
  1342.5 506.4 %copy-start.7 = (f32[64,32,16]{2,1,0:T(8,128)S(1)}, f32[64,32,16]{2,1,0:T(8,128)}, u32[]{:S(2)}) copy-start(f32[64,32,16]{2,1,0:T(8,128)} %get-tuple-element.1048) | copy-start | bytes 393220
  2046.6 5.0 collective-permute-start.11
  2050.2 4.3 collective-permute-start.12
  2058.9 200.0 %all-to-all-start.7 = ((f32[64,6,1,256]{3,2,1,0:T(1,128)}), f32[64,6,1,256]{3,2,1,0:T(1,128)S(1)}, u32[]{:S(2)}, u32[]{:S(2)}) async-start(f32[64,6,1,256]{3,2,1,0:T(1,128)} %broadcast_in_dim.222), calls=%async_computation.7 | async-start | bytes 786432 | tf_op jit(solution)/shard_map/all_to_all | solution.py:40
  2264.7 12.2 collective-permute-start.13
  2275.4 4.6 collective-permute-start.14
  2326.1 5.0 collective-permute-start.15
  2329.8 4.4 collective-permute-start.16
  2343.8 13.5 all-to-all-start.12
  2364.8 14.9 all-to-all-start.13
  (200 other events, 2178.5 us)
